TPU v7x, 512 devices: a whole 4x8x8 slice. The times are simulated.
512 devices in a mesh: group: 8 (over z_lo, core), dp: 8 (over y), tensor: 8 (over z_hi, x).
Axes of the slice: x: 4, y: 8, z: 8 (z_hi: 2, z_lo: 4; z = z_hi * 4 + z_lo), core: 2. Of those that a mesh axis runs over, the one named last changes fastest.
Arguments:
- keyvalue_local: float32 [8, 2, 4096, 1024], P('group', None, 'dp', 'tensor'), may hold values from -6 to 6
- keyvalue_anchor: float32 [2, 4096, 1024], P(None, 'dp', 'tensor'), may hold values from -6 to 6
- keyvalue_state: float32 [2, 4096, 1024], P(None, 'dp', 'tensor'), may hold values from -6 to 6
- router_local: float32 [8, 4096, 8], P('group', 'dp'), may hold values from -6 to 6
- router_anchor: float32 [4096, 8], P('dp'), may hold values from -6 to 6
- router_state: float32 [4096, 8], P('dp'), may hold values from -6 to 6
- gain_local: float32 [8, 2, 4096], P('group', None, 'dp'), may hold values from -6 to 6
- gain_anchor: float32 [2, 4096], P(None, 'dp'), may hold values from -6 to 6
- gain_state: float32 [2, 4096], P(None, 'dp'), may hold values from -6 to 6
- embed_local: float32 [8, 1000, 4096], P('group', 'dp', 'tensor'), may hold values from -6 to 6
- embed_anchor: float32 [1000, 4096], P('dp', 'tensor'), may hold values from -6 to 6
- embed_state: float32 [1000, 4096], P('dp', 'tensor'), may hold values from -6 to 6
- embed_basis: float32 [4096, 64], P('tensor'), may hold values from -0.25 to 0.25
- outer_rate: float32 [], replicated, may hold values from 0.5 to 1
Outputs:
- keyvalue_average: float32 [2, 4096, 1024], P(None, 'dp', 'tensor')
- keyvalue_momentum: float32 [2, 4096, 1024], P(None, 'dp', 'tensor')
- keyvalue_updated: float32 [2, 4096, 1024], P(None, 'dp', 'tensor')
- router_average: float32 [4096, 8], P('dp')
- router_momentum: float32 [4096, 8], P('dp')
- router_updated: float32 [4096, 8], P('dp')
- gain_average: float32 [2, 4096], P(None, 'dp')
- gain_momentum: float32 [2, 4096], P(None, 'dp')
- gain_updated: float32 [2, 4096], P(None, 'dp')
- embed_average: float32 [1000, 4096], P('dp', 'tensor')
- embed_momentum: float32 [1000, 4096], P('dp', 'tensor')
- embed_updated: float32 [1000, 4096], P('dp', 'tensor')
All inputs are finite; a program needn't handle non-finite values.
Results may differ from a plain program's by a relative error of at most 0.0001.
Values sent between devices are 32-bit elements; how exact they have to be, the bound alone decides.
No kernel may reach another device: no remote copies, remote signals or barrier semaphores. Data moves between devices by JAX's collectives and lax.ppermute only.
A program may use at most 64 MiB of HBM per device.

v0:
```python
import jax
import jax.numpy as jnp
from jax import lax
from jax.sharding import PartitionSpec as P


def nesterov(average, state, anchor, outer_rate):
    momentum = 0.5 * state + average
    updated = anchor - outer_rate * (average + 0.5 * momentum)
    return (average, momentum, updated)


def owned_slice(whole, position, count, axis_dim):
    return lax.dynamic_slice_in_dim(whole, position * count, count, axis_dim)


def local(
    keyvalue_local,
    keyvalue_anchor,
    keyvalue_state,
    router_local,
    router_anchor,
    router_state,
    gain_local,
    gain_anchor,
    gain_state,
    embed_local,
    embed_anchor,
    embed_state,
    embed_basis,
    outer_rate,
):
    groups = lax.axis_size("group")
    keyvalue_diff = keyvalue_anchor - keyvalue_local[0]
    router_diff = router_anchor - router_local[0]
    gain_diff = gain_anchor - gain_local[0]
    keyvalue_sum, router_sum, gain_sum = (
        lax.psum_scatter(keyvalue_diff, "group", scatter_dimension=1, tiled=True),
        lax.psum_scatter(router_diff, "group", scatter_dimension=0, tiled=True),
        lax.psum_scatter(gain_diff, "group", scatter_dimension=1, tiled=True),
    )
    position = lax.axis_index("group")
    keyvalue_rows = keyvalue_anchor.shape[1] // groups
    router_rows = router_anchor.shape[0] // groups
    gain_rows = gain_anchor.shape[1] // groups
    keyvalue_part = nesterov(
        keyvalue_sum / groups,
        owned_slice(keyvalue_state, position, keyvalue_rows, 1),
        owned_slice(keyvalue_anchor, position, keyvalue_rows, 1),
        outer_rate,
    )
    router_part = nesterov(
        router_sum / groups,
        owned_slice(router_state, position, router_rows, 0),
        owned_slice(router_anchor, position, router_rows, 0),
        outer_rate,
    )
    gain_part = nesterov(
        gain_sum / groups,
        owned_slice(gain_state, position, gain_rows, 1),
        owned_slice(gain_anchor, position, gain_rows, 1),
        outer_rate,
    )
    gathered = (
        lax.all_gather(keyvalue_part[0], "group", axis=1, tiled=True),
        lax.all_gather(keyvalue_part[1], "group", axis=1, tiled=True),
        lax.all_gather(keyvalue_part[2], "group", axis=1, tiled=True),
        lax.all_gather(router_part[0], "group", axis=0, tiled=True),
        lax.all_gather(router_part[1], "group", axis=0, tiled=True),
        lax.all_gather(router_part[2], "group", axis=0, tiled=True),
        lax.all_gather(gain_part[0], "group", axis=1, tiled=True),
        lax.all_gather(gain_part[1], "group", axis=1, tiled=True),
        lax.all_gather(gain_part[2], "group", axis=1, tiled=True),
    )
    keyvalue_out = gathered[0:3]
    router_out = gathered[3:6]
    gain_out = gathered[6:9]
    partial_factors = jnp.dot(
        embed_anchor - embed_local[0],
        embed_basis,
        precision=lax.Precision.HIGHEST,
        preferred_element_type=jnp.float32,
    )
    factors = lax.psum(partial_factors, ("group", "tensor"))
    factors = factors / groups
    embed_average = jnp.dot(
        factors, embed_basis.T, precision=lax.Precision.HIGHEST, preferred_element_type=jnp.float32
    )
    embed_out = nesterov(embed_average, embed_state, embed_anchor, outer_rate)
    return (
        keyvalue_out[0],
        keyvalue_out[1],
        keyvalue_out[2],
        router_out[0],
        router_out[1],
        router_out[2],
        gain_out[0],
        gain_out[1],
        gain_out[2],
        embed_out[0],
        embed_out[1],
        embed_out[2],
    )


def solution(mesh):
    in_specs = (
        P("group", None, "dp", "tensor"),
        P(None, "dp", "tensor"),
        P(None, "dp", "tensor"),
        P("group", "dp", None),
        P("dp", None),
        P("dp", None),
        P("group", None, "dp"),
        P(None, "dp"),
        P(None, "dp"),
        P("group", "dp", "tensor"),
        P("dp", "tensor"),
        P("dp", "tensor"),
        P("tensor", None),
        P(),
    )
    out_specs = (
        P(None, "dp", "tensor"),
        P(None, "dp", "tensor"),
        P(None, "dp", "tensor"),
        P("dp", None),
        P("dp", None),
        P("dp", None),
        P(None, "dp"),
        P(None, "dp"),
        P(None, "dp"),
        P("dp", "tensor"),
        P("dp", "tensor"),
        P("dp", "tensor"),
    )
    return jax.shard_map(local, mesh=mesh, in_specs=in_specs, out_specs=out_specs, check_vma=False)
```

profile of v0, /device:TPU:63, one launch (start us, length us, event | category | flops | bytes accessed | tf_op | source)
XLA Modules:
  0.0 511.7 jit_solution(6677557871619569564)
XLA Ops:
  7.3 0.7 bitcast_subtract_fusion.4
  8.0 0.9 copy.46
  9.0 0.8 copy.44
  9.9 0.8 bitcast_subtract_fusion
  12.2 342.6 %psum.7 = f32[125,64]{0,1:T(8,128)S(1)} all-reduce(f32[125,64]{0,1:T(8,128)S(1)} %fusion), channel_id=1, replica_groups=mesh['group'=8,'dp'=8,'tensor'=8] {'group','tensor'}, use_global_device_ids=true, to_apply=%region_3.0 | all-reduce | flops 8000 | bytes 64000 | tf_op jit(solution)/shard_map/psum | solution.py:84
  354.8 1.3 multiply_subtract_fusion
  356.1 0.8 copy.47
  356.9 0.8 fusion.9
  357.7 32.8 %all-gather.5 = f32[8,64,2]{1,2,0:T(2,128)S(1)} all-gather(f32[1,64,2]{1,2,0:T(2,128)S(1)} %get-tuple-element.19), channel_id=1, replica_groups=mesh['group'=8,'dp'=8,'tensor'=8] {'group'}, dimensions={0}, use_global_device_ids=true | all-gather | bytes 4608 | tf_op jit(solution)/shard_map/all_gather | solution.py:73
  391.2 8.7 %all-gather.4 = f32[8,64,2]{1,2,0:T(2,128)S(1)} all-gather(f32[1,64,2]{1,2,0:T(2,128)S(1)} %get-tuple-element.20), channel_id=1, replica_groups=mesh['group'=8,'dp'=8,'tensor'=8] {'group'}, dimensions={0}, use_global_device_ids=true | all-gather | bytes 4608 | tf_op jit(solution)/shard_map/all_gather | solution.py:72
  400.6 10.1 %all-gather.3 = f32[8,64,2]{1,2,0:T(2,128)S(1)} all-gather(f32[1,64,2]{1,2,0:T(2,128)S(1)} %get-tuple-element.22), channel_id=1, replica_groups=mesh['group'=8,'dp'=8,'tensor'=8] {'group'}, dimensions={0}, use_global_device_ids=true | all-gather | bytes 4608 | tf_op jit(solution)/shard_map/all_gather | solution.py:71
  411.3 0.8 copy.45
  412.1 0.8 subtract_bitcast_fusion
  412.9 14.1 %all-gather.2 = f32[8,64,8]{1,2,0:T(8,128)S(1)} all-gather(f32[1,64,8]{1,2,0:T(8,128)S(1)} %get-tuple-element.17), channel_id=1, replica_groups=mesh['group'=8,'dp'=8,'tensor'=8] {'group'}, dimensions={0}, use_global_device_ids=true | all-gather | bytes 18432 | tf_op jit(solution)/shard_map/all_gather | solution.py:70
  427.7 14.1 %all-gather.1 = f32[8,64,8]{1,2,0:T(8,128)S(1)} all-gather(f32[1,64,8]{1,2,0:T(8,128)S(1)} %get-tuple-element.18), channel_id=1, replica_groups=mesh['group'=8,'dp'=8,'tensor'=8] {'group'}, dimensions={0}, use_global_device_ids=true | all-gather | bytes 18432 | tf_op jit(solution)/shard_map/all_gather | solution.py:69
  441.7 0.7 reshape.27
  442.4 14.1 %all-gather = f32[8,64,8]{1,2,0:T(8,128)S(1)} all-gather(f32[1,64,8]{1,2,0:T(8,128)S(1)} %get-tuple-element.21), channel_id=1, replica_groups=mesh['group'=8,'dp'=8,'tensor'=8] {'group'}, dimensions={0}, use_global_device_ids=true | all-gather | bytes 18432 | tf_op jit(solution)/shard_map/all_gather | solution.py:68
  457.2 0.9 multiply_subtract_fusion.1
  458.1 14.9 %all_gather.29 = f32[2,512,128]{2,1,0:T(8,128)S(1)} all-gather(f32[2,64,128]{2,1,0:T(8,128)S(1)} %get-tuple-element.14), channel_id=1, replica_groups=mesh['group'=8,'dp'=8,'tensor'=8] {'group'}, dimensions={1}, use_global_device_ids=true | all-gather | bytes 589824 | tf_op jit(solution)/shard_map/all_gather | solution.py:67
  473.0 14.9 %all_gather.28 = f32[2,512,128]{2,1,0:T(8,128)S(1)} all-gather(f32[2,64,128]{2,1,0:T(8,128)S(1)} %get-tuple-element.15), channel_id=1, replica_groups=mesh['group'=8,'dp'=8,'tensor'=8] {'group'}, dimensions={1}, use_global_device_ids=true | all-gather | bytes 589824 | tf_op jit(solution)/shard_map/all_gather | solution.py:66
  487.9 14.9 %all_gather.27 = f32[2,512,128]{2,1,0:T(8,128)S(1)} all-gather(f32[2,64,128]{2,1,0:T(8,128)S(1)} %get-tuple-element.16), channel_id=1, replica_groups=mesh['group'=8,'dp'=8,'tensor'=8] {'group'}, dimensions={1}, use_global_device_ids=true | all-gather | bytes 589824 | tf_op jit(solution)/shard_map/all_gather | solution.py:65
  502.8 0.8 copy.57
  503.6 0.8 copy.58
  504.4 0.8 copy.59
  (38 shorter events, 4.3 us)
Async XLA Ops:
  7.2 4.3 copy-start
  7.2 348.9 %reduce-scatter.12.cloned.1.call-start = ((), (), s32[]{:S(2)}) async-start(), calls=%async_computation.5 | async-start | bytes 294912
  7.2 1.7 copy-start.6
  7.2 1.7 copy-start.7
  8.0 1.9 copy-start.2
  8.0 1.9 copy-start.3
  8.9 402.4 %reduce-scatter.10.cloned.1.call-start = ((), (), s32[]{:S(2)}) async-start(), calls=%async_computation.4 | async-start | bytes 294912
  9.8 447.4 %reduce-scatter.8.cloned.1.call-start = ((), (), s32[]{:S(2)}) async-start(), calls=%async_computation.3 | async-start | bytes 589824 | tf_op jit(solution)/shard_map/reduce_scatter | solution.py:38
  10.8 0.9 copy-start.1
  10.8 1.0 copy-start.4
  11.8 343.0 %copy-start.5 = (f32[125,512]{1,0:T(8,128)S(1)}, f32[125,512]{1,0:T(8,128)}, u32[]{:S(2)}) copy-start(f32[125,512]{1,0:T(8,128)} %param.25) | copy-start | bytes 768004
Sparse Core Ops, SparseCore 0:
  11.4 40.1 reduce-scatter.11
  54.9 37.6 reduce-scatter.9
  96.0 38.3 reduce-scatter.7
where the time goes:
time: 512 us
  blocking collectives  481 us (94%)
  between operations  14.6 us (3%)
  local copies, waits for them, and re-layouts  10.1 us (2%)
    psum x1, blocking collectives, local(): factors = lax.psum(partial_factors, ('group', 'tensor'))  343 us
    all_gather x1, blocking collectives, local(): lax.all_gather(gain_part[2], 'group', axis=1, tiled=True)  32.8 us
    all_gather x1, blocking collectives, local(): lax.all_gather(keyvalue_part[2], 'group', axis=1, tiled=True)  14.9 us
    all_gather x1, blocking collectives, local(): lax.all_gather(keyvalue_part[1], 'group', axis=1, tiled=True)  14.9 us
    all_gather x1, blocking collectives, local(): lax.all_gather(keyvalue_part[0], 'group', axis=1, tiled=True)  14.9 us
    all_gather x1, blocking collectives, local(): lax.all_gather(router_part[2], 'group', axis=0, tiled=True)  14.1 us
    all_gather x1, blocking collectives, local(): lax.all_gather(router_part[0], 'group', axis=0, tiled=True)  14.1 us
    all_gather x1, blocking collectives, local(): lax.all_gather(router_part[1], 'group', axis=0, tiled=True)  14.1 us
  transfers between devices with their start and end apart: 3, of which 0 were waited for; matrix products, arithmetic and copies ran while one was open for 2% of the time, Pallas kernels for 0%

commit v1 on v0

--- a/solution.py
+++ b/solution.py
@@ -81,7 +81,7 @@
         precision=lax.Precision.HIGHEST,
         preferred_element_type=jnp.float32,
     )
-    factors = lax.psum(partial_factors, ("group", "tensor"))
+    factors = jnp.sum(lax.all_gather(partial_factors, ("group", "tensor")), axis=0)
     factors = factors / groups
     embed_average = jnp.dot(
         factors, embed_basis.T, precision=lax.Precision.HIGHEST, preferred_element_type=jnp.float32

time: 512 us -> 227 us (0.44)
  the two profiles are of different devices: /device:TPU:63 before, /device:TPU:128 now
where the time goes in v1:
time: 227 us; the launch traced here: 226 us
  blocking collectives  122 us (54%)
  waiting for transfers between devices  67.8 us (30%)
  between operations  15.9 us (7%)
  local copies, waits for them, and re-layouts  9.82 us (4%)
  other arithmetic  7.87 us (3%)
  matrix products  2.35 us (1%)
    unnamed x6, waiting for transfers between devices  40.2 us
    all_gather x1, waiting for transfers between devices, local(): lax.all_gather(partial_factors, ('group', 'tensor'))  27.6 us
    all_gather x1, blocking collectives, local(): lax.all_gather(router_part[2], 'group', axis=0, tiled=True)  18.1 us
    all_gather x1, blocking collectives, local(): lax.all_gather(keyvalue_part[1], 'group', axis=1, tiled=True)  15.3 us
    all_gather x1, blocking collectives, local(): lax.all_gather(keyvalue_part[0], 'group', axis=1, tiled=True)  15.2 us
    all_gather x1, blocking collectives, local(): lax.all_gather(keyvalue_part[2], 'group', axis=1, tiled=True)  15 us
    all_gather x1, blocking collectives, local(): lax.all_gather(router_part[0], 'group', axis=0, tiled=True)  14.1 us
    all_gather x1, blocking collectives, local(): lax.all_gather(router_part[1], 'group', axis=0, tiled=True)  14.1 us
  transfers between devices with their start and end apart: 4, of which 3 were waited for; matrix products, arithmetic and copies ran while one was open for 6% of the time, Pallas kernels for 0%

profile of v1, /device:TPU:128, one launch (start us, length us, event | category | flops | bytes accessed | tf_op | source)
XLA Modules:
  0.0 226.4 jit_solution(5394918467994137667)
XLA Ops:
  8.9 0.9 copy.46
  10.5 0.8 copy.44
  11.5 2.0 bitcast_subtract_fusion
  13.6 1.0 convolution_bitcast_fusion
  15.3 33.2 %reduce-scatter.12.cloned.1.call-done = f32[64,2]{1,0:T(8,128)} async-done(((f32[512,2]{1,0:T(8,128)}), f32[64,2]{1,0:T(8,128)}) %reduce-scatter.12.cloned.1.call-update) | async-done | bytes 528
  48.5 0.8 copy.47
  50.1 11.9 %all-gather.6 = f32[8,64,2]{1,2,0:T(2,128)S(1)} all-gather(f32[1,64,2]{1,2,0:T(2,128)S(1)} %get-tuple-element.19), channel_id=1, replica_groups=mesh['group'=8,'dp'=8,'tensor'=8] {'group'}, dimensions={0}, use_global_device_ids=true | all-gather | bytes 4608 | tf_op jit(solution)/shard_map/all_gather | solution.py:73
  62.6 10.1 %all-gather.5 = f32[8,64,2]{1,2,0:T(2,128)S(1)} all-gather(f32[1,64,2]{1,2,0:T(2,128)S(1)} %get-tuple-element.20), channel_id=1, replica_groups=mesh['group'=8,'dp'=8,'tensor'=8] {'group'}, dimensions={0}, use_global_device_ids=true | all-gather | bytes 4608 | tf_op jit(solution)/shard_map/all_gather | solution.py:72
  73.3 8.8 %all-gather.4 = f32[8,64,2]{1,2,0:T(2,128)S(1)} all-gather(f32[1,64,2]{1,2,0:T(2,128)S(1)} %get-tuple-element.22), channel_id=1, replica_groups=mesh['group'=8,'dp'=8,'tensor'=8] {'group'}, dimensions={0}, use_global_device_ids=true | all-gather | bytes 4608 | tf_op jit(solution)/shard_map/all_gather | solution.py:71
  82.8 7.0 %reduce-scatter.10.cloned.1.call-done = f32[64,8]{1,0:T(8,128)} async-done(((f32[512,8]{1,0:T(8,128)}), f32[64,8]{1,0:T(8,128)}) %reduce-scatter.10.cloned.1.call-update) | async-done | bytes 2064
  89.8 0.8 copy.45
  91.4 18.1 %all-gather.3 = f32[8,64,8]{1,2,0:T(8,128)S(1)} all-gather(f32[1,64,8]{1,2,0:T(8,128)S(1)} %get-tuple-element.17), channel_id=1, replica_groups=mesh['group'=8,'dp'=8,'tensor'=8] {'group'}, dimensions={0}, use_global_device_ids=true | all-gather | bytes 18432 | tf_op jit(solution)/shard_map/all_gather | solution.py:70
  110.2 14.1 %all-gather.2 = f32[8,64,8]{1,2,0:T(8,128)S(1)} all-gather(f32[1,64,8]{1,2,0:T(8,128)S(1)} %get-tuple-element.18), channel_id=1, replica_groups=mesh['group'=8,'dp'=8,'tensor'=8] {'group'}, dimensions={0}, use_global_device_ids=true | all-gather | bytes 18432 | tf_op jit(solution)/shard_map/all_gather | solution.py:69
  125.0 14.1 %all-gather.1 = f32[8,64,8]{1,2,0:T(8,128)S(1)} all-gather(f32[1,64,8]{1,2,0:T(8,128)S(1)} %get-tuple-element.21), channel_id=1, replica_groups=mesh['group'=8,'dp'=8,'tensor'=8] {'group'}, dimensions={0}, use_global_device_ids=true | all-gather | bytes 18432 | tf_op jit(solution)/shard_map/all_gather | solution.py:68
  139.7 1.0 multiply_subtract_fusion.1
  140.7 15.0 %all_gather.35 = f32[2,512,128]{2,1,0:T(8,128)S(1)} all-gather(f32[2,64,128]{2,1,0:T(8,128)S(1)} %get-tuple-element.14), channel_id=1, replica_groups=mesh['group'=8,'dp'=8,'tensor'=8] {'group'}, dimensions={1}, use_global_device_ids=true | all-gather | bytes 589824 | tf_op jit(solution)/shard_map/all_gather | solution.py:67
  155.7 15.3 %all_gather.34 = f32[2,512,128]{2,1,0:T(8,128)S(1)} all-gather(f32[2,64,128]{2,1,0:T(8,128)S(1)} %get-tuple-element.15), channel_id=1, replica_groups=mesh['group'=8,'dp'=8,'tensor'=8] {'group'}, dimensions={1}, use_global_device_ids=true | all-gather | bytes 589824 | tf_op jit(solution)/shard_map/all_gather | solution.py:66
  171.0 15.2 %all_gather.33 = f32[2,512,128]{2,1,0:T(8,128)S(1)} all-gather(f32[2,64,128]{2,1,0:T(8,128)S(1)} %get-tuple-element.16), channel_id=1, replica_groups=mesh['group'=8,'dp'=8,'tensor'=8] {'group'}, dimensions={1}, use_global_device_ids=true | all-gather | bytes 589824 | tf_op jit(solution)/shard_map/all_gather | solution.py:65
  186.2 27.6 %all-gather.10.cloned.1.call-done = f32[64,125,64]{1,2,0:T(8,128)} async-done(((f32[1,125,64]{1,2,0:T(8,128)}), f32[64,125,64]{1,2,0:T(8,128)}) %all-gather.10.cloned.1.call-update) | async-done | bytes 2048016 | tf_op jit(solution)/shard_map/all_gather | solution.py:84
  213.8 1.8 reduce_sum.9
  215.6 1.3 multiply_subtract_fusion
  216.9 0.8 copy.57
  217.7 0.8 copy.58
  218.5 0.8 copy.59
  (33 shorter events, 7.4 us)
Async XLA Ops:
  8.0 5.6 %copy-start = (f32[512,64]{0,1:T(8,128)S(1)}, f32[512,64]{0,1:T(8,128)}, u32[]{:S(2)}) copy-start(f32[512,64]{0,1:T(8,128)} %param.26) | copy-start | bytes 393220
  8.0 5.6 %copy-start.1 = (f32[125,512]{1,0:T(8,128)S(1)}, f32[125,512]{1,0:T(8,128)}, u32[]{:S(2)}) copy-start(f32[125,512]{1,0:T(8,128)} %param.24) | copy-start | bytes 768004
  8.0 5.6 %copy-start.2 = (f32[1,125,512]{2,0,1:T(1,128)S(1)}, f32[1,125,512]{2,0,1:T(1,128)}, u32[]{:S(2)}) copy-start(f32[1,125,512]{2,0,1:T(1,128)} %param.23) | copy-start | bytes 768004
  8.0 40.4 %reduce-scatter.12.cloned.1.call-start = ((), (), s32[]{:S(2)}) async-start(), calls=%async_computation.6 | async-start | bytes 294912
  9.7 80.0 %reduce-scatter.10.cloned.1.call-start = ((), (), s32[]{:S(2)}) async-start(), calls=%async_computation.5 | async-start | bytes 294912
  11.4 128.3 %reduce-scatter.8.cloned.1.call-start = ((), (), s32[]{:S(2)}) async-start(), calls=%async_computation.3 | async-start | bytes 589824 | tf_op jit(solution)/shard_map/reduce_scatter | solution.py:38
  13.5 200.3 %all-gather.10.cloned.1.call-start = ((), (), s32[]{:S(2)}) async-start(), calls=%async_computation.4 | async-start | bytes 2129920 | tf_op jit(solution)/shard_map/all_gather | solution.py:84
  139.7 75.8 %copy-start.3 = (f32[125,512]{1,0:T(8,128)S(1)}, f32[125,512]{1,0:T(8,128)}, u32[]{:S(2)}) copy-start(f32[125,512]{1,0:T(8,128)} %param.25) | copy-start | bytes 768004
Sparse Core Ops, SparseCore 0:
  12.2 36.1 reduce-scatter.11
  51.8 37.9 reduce-scatter.9
  93.1 38.0 reduce-scatter.7
Sparse Core Ops, SparseCore 1:
  16.7 197.0 all-gather.9

commit v2 on v0

--- a/solution.py
+++ b/solution.py
@@ -62,7 +62,10 @@
         outer_rate,
     )
     gathered = (
-        lax.all_gather(keyvalue_part[0], "group", axis=1, tiled=True),
+        jnp.concatenate(
+            lax.all_to_all(jnp.stack([keyvalue_part[0]] * lax.axis_size("group")), "group", 0, 0),
+            axis=1,
+        ),
         lax.all_gather(keyvalue_part[1], "group", axis=1, tiled=True),
         lax.all_gather(keyvalue_part[2], "group", axis=1, tiled=True),
         lax.all_gather(router_part[0], "group", axis=0, tiled=True),

time: 512 us -> 509 us (level)
  the two profiles are of different devices: /device:TPU:63 before, /device:TPU:31 now
where the time goes in v2:
time: 509 us
  blocking collectives  450 us (88%)
  starting transfers between devices  25.8 us (5%)
  between operations  14.5 us (3%)
  local copies, waits for them, and re-layouts  11.4 us (2%)
  other arithmetic  5.12 us (1%)
    psum x1, blocking collectives, local(): factors = lax.psum(partial_factors, ('group', 'tensor'))  343 us
    all_to_all x1, starting transfers between devices, local(): lax.all_to_all(jnp.stack([keyvalue_part[0]] * lax.axis_size('group')), 'g...  25.7 us
    all_gather x1, blocking collectives, local(): lax.all_gather(gain_part[2], 'group', axis=1, tiled=True)  15.3 us
    all_gather x1, blocking collectives, local(): lax.all_gather(keyvalue_part[1], 'group', axis=1, tiled=True)  14.8 us
    all_gather x1, blocking collectives, local(): lax.all_gather(keyvalue_part[2], 'group', axis=1, tiled=True)  14.8 us
    all_gather x1, blocking collectives, local(): lax.all_gather(router_part[2], 'group', axis=0, tiled=True)  14.1 us
    all_gather x1, blocking collectives, local(): lax.all_gather(router_part[1], 'group', axis=0, tiled=True)  14.1 us
    all_gather x1, blocking collectives, local(): lax.all_gather(router_part[0], 'group', axis=0, tiled=True)  14.1 us
  transfers between devices with their start and end apart: 4, of which 0 were waited for; matrix products, arithmetic and copies ran while one was open for 3% of the time, Pallas kernels for 0%

profile of v2, /device:TPU:31, one launch (start us, length us, event | category | flops | bytes accessed | tf_op | source)
XLA Modules:
  0.0 508.8 jit_solution(12624684738381875045)
XLA Ops:
  7.2 0.8 bitcast_subtract_fusion.4
  8.0 0.9 copy.47
  9.0 1.9 bitcast_subtract_fusion
  11.6 0.8 copy.45
  13.6 342.6 %psum.7 = f32[125,64]{0,1:T(8,128)S(1)} all-reduce(f32[125,64]{0,1:T(8,128)S(1)} %fusion), channel_id=1, replica_groups=mesh['group'=8,'dp'=8,'tensor'=8] {'group','tensor'}, use_global_device_ids=true, to_apply=%region_3.0 | all-reduce | flops 8000 | bytes 64000 | tf_op jit(solution)/shard_map/psum | solution.py:87
  356.2 1.3 multiply_subtract_fusion
  357.5 0.8 copy.48
  358.3 0.9 multiply_subtract_fusion.1
  359.2 0.8 stack.2
  360.1 25.7 %all-to-all-start = ((f32[8,2,64,128]{3,2,1,0:T(8,128)}), f32[8,2,64,128]{3,2,1,0:T(8,128)S(1)}, u32[]{:S(2)}, u32[]{:S(2)}) async-start(f32[8,2,64,128]{3,2,1,0:T(8,128)} %stack.2), calls=%async_computation.1 | async-start | bytes 1048576 | tf_op jit(solution)/shard_map/all_to_all | solution.py:66
  385.8 0.8 fusion.9
  386.5 15.3 %all-gather.5 = f32[8,64,2]{1,2,0:T(2,128)S(1)} all-gather(f32[1,64,2]{1,2,0:T(2,128)S(1)} %get-tuple-element.19), channel_id=1, replica_groups=mesh['group'=8,'dp'=8,'tensor'=8] {'group'}, dimensions={0}, use_global_device_ids=true | all-gather | bytes 4608 | tf_op jit(solution)/shard_map/all_gather | solution.py:76
  402.5 11.8 %all-gather.4 = f32[8,64,2]{1,2,0:T(2,128)S(1)} all-gather(f32[1,64,2]{1,2,0:T(2,128)S(1)} %get-tuple-element.20), channel_id=1, replica_groups=mesh['group'=8,'dp'=8,'tensor'=8] {'group'}, dimensions={0}, use_global_device_ids=true | all-gather | bytes 4608 | tf_op jit(solution)/shard_map/all_gather | solution.py:75
  414.9 8.7 %all-gather.3 = f32[8,64,2]{1,2,0:T(2,128)S(1)} all-gather(f32[1,64,2]{1,2,0:T(2,128)S(1)} %get-tuple-element.22), channel_id=1, replica_groups=mesh['group'=8,'dp'=8,'tensor'=8] {'group'}, dimensions={0}, use_global_device_ids=true | all-gather | bytes 4608 | tf_op jit(solution)/shard_map/all_gather | solution.py:74
  424.3 0.8 copy.46
  425.1 0.8 subtract_bitcast_fusion
  425.9 14.1 %all-gather.2 = f32[8,64,8]{1,2,0:T(8,128)S(1)} all-gather(f32[1,64,8]{1,2,0:T(8,128)S(1)} %get-tuple-element.17), channel_id=1, replica_groups=mesh['group'=8,'dp'=8,'tensor'=8] {'group'}, dimensions={0}, use_global_device_ids=true | all-gather | bytes 18432 | tf_op jit(solution)/shard_map/all_gather | solution.py:73
  440.7 14.1 %all-gather.1 = f32[8,64,8]{1,2,0:T(8,128)S(1)} all-gather(f32[1,64,8]{1,2,0:T(8,128)S(1)} %get-tuple-element.18), channel_id=1, replica_groups=mesh['group'=8,'dp'=8,'tensor'=8] {'group'}, dimensions={0}, use_global_device_ids=true | all-gather | bytes 18432 | tf_op jit(solution)/shard_map/all_gather | solution.py:72
  455.4 14.1 %all-gather = f32[8,64,8]{1,2,0:T(8,128)S(1)} all-gather(f32[1,64,8]{1,2,0:T(8,128)S(1)} %get-tuple-element.21), channel_id=1, replica_groups=mesh['group'=8,'dp'=8,'tensor'=8] {'group'}, dimensions={0}, use_global_device_ids=true | all-gather | bytes 18432 | tf_op jit(solution)/shard_map/all_gather | solution.py:71
  470.2 14.8 %all_gather.25 = f32[2,512,128]{2,1,0:T(8,128)S(1)} all-gather(f32[2,64,128]{2,1,0:T(8,128)S(1)} %get-tuple-element.14), channel_id=1, replica_groups=mesh['group'=8,'dp'=8,'tensor'=8] {'group'}, dimensions={1}, use_global_device_ids=true | all-gather | bytes 589824 | tf_op jit(solution)/shard_map/all_gather | solution.py:70
  485.0 14.8 %all_gather.24 = f32[2,512,128]{2,1,0:T(8,128)S(1)} all-gather(f32[2,64,128]{2,1,0:T(8,128)S(1)} %get-tuple-element.15), channel_id=1, replica_groups=mesh['group'=8,'dp'=8,'tensor'=8] {'group'}, dimensions={1}, use_global_device_ids=true | all-gather | bytes 589824 | tf_op jit(solution)/shard_map/all_gather | solution.py:69
  499.8 0.8 copy.38
  500.7 0.8 copy.57
  501.5 0.8 copy.58
  (38 shorter events, 5.3 us)
Async XLA Ops:
  7.2 5.9 %copy-start = (f32[512,64]{0,1:T(8,128)S(1)}, f32[512,64]{0,1:T(8,128)}, u32[]{:S(2)}) copy-start(f32[512,64]{0,1:T(8,128)} %param.26) | copy-start | bytes 393220
  7.2 1.8 copy-start.2
  7.2 350.3 %reduce-scatter.12.cloned.1.call-start = ((), (), s32[]{:S(2)}) async-start(), calls=%async_computation.6 | async-start | bytes 294912
  8.9 349.4 %reduce-scatter.8.cloned.1.call-start = ((), (), s32[]{:S(2)}) async-start(), calls=%async_computation.4 | async-start | bytes 589824 | tf_op jit(solution)/shard_map/reduce_scatter | solution.py:38
  10.9 0.7 copy-start.5
  10.9 0.7 copy-start.6
  10.9 413.4 %reduce-scatter.10.cloned.1.call-start = ((), (), s32[]{:S(2)}) async-start(), calls=%async_computation.5 | async-start | bytes 294912
  11.6 1.5 copy-start.1
  11.6 1.5 copy-start.3
  13.2 343.0 %copy-start.4 = (f32[125,512]{1,0:T(8,128)S(1)}, f32[125,512]{1,0:T(8,128)}, u32[]{:S(2)}) copy-start(f32[125,512]{1,0:T(8,128)} %param.25) | copy-start | bytes 768004
  360.1 139.7 %all-to-all-start = ((f32[8,2,64,128]{3,2,1,0:T(8,128)}), f32[8,2,64,128]{3,2,1,0:T(8,128)S(1)}, u32[]{:S(2)}, u32[]{:S(2)}) async-start(f32[8,2,64,128]{3,2,1,0:T(8,128)} %stack.2), calls=%async_computation.1 | async-start | bytes 1048576 | tf_op jit(solution)/shard_map/all_to_all | solution.py:66
Sparse Core Ops, SparseCore 0:
  11.4 40.4 reduce-scatter.11
  55.2 38.1 reduce-scatter.7
  96.8 37.6 reduce-scatter.9
